TPU v7x, 32 devices: a whole 2x2x4 slice. The times are simulated.
32 devices in a mesh: dp: 4 (over z), space: 4 (over x, core), rep: 2 (over y).
Axes of the slice: x: 2, y: 2, z: 4, core: 2. Of those that a mesh axis runs over, the one named last changes fastest.
Arguments:
- frames: bfloat16 [6, 8, 32, 32, 512], P(None, ('dp', 'rep'), 'space'), may hold values from -6 to 6
- membrane: bfloat16 [8, 32, 32, 512], P(('dp', 'rep'), 'space'), may hold values from -6 to 6
- cotangent: bfloat16 [6, 8, 32, 32, 512], P(None, ('dp', 'rep'), 'space'), may hold values from -6 to 6
- master: float32 [4608, 512], P('dp'), may hold values from -0.09375 to 0.09375
- moment: float32 [4608, 512], P('dp'), may hold values from -4 to 4
- second: float32 [4608, 512], P('dp'), may hold values from 0.05 to 5
Outputs:
- grad_input: bfloat16 [6, 8, 32, 32, 512], P(None, ('dp', 'rep'), 'space')
- membrane_grad: float32 [8, 32, 32, 512], P(('dp', 'rep'), 'space')
- weight_grad: float32 [4608, 512], P('dp')
- new_moment: float32 [4608, 512], P('dp')
- new_second: float32 [4608, 512], P('dp')
- update: float32 [4608, 512], P('dp')
All inputs are finite; a program needn't handle non-finite values.
Results may differ from a plain program's by a relative error of at most 0.003.
Values may be sent and summed in bfloat16 or wider, within the bound.
No kernel may reach another device: no remote copies, remote signals or barrier semaphores. Data moves between devices by JAX's collectives and lax.ppermute only.
A program may use at most 192 MiB of HBM per device.

v0:
```python
import math
import jax
import jax.numpy as jnp
from jax import lax
from jax.sharding import PartitionSpec as P


def extended(x, sides, width):
    for axis, dim in sides:
        peers, length = (lax.axis_size(axis), x.shape[dim])
        up = [(i, (i + 1) % peers) for i in range(peers - 1)]
        down = [(j, i) for i, j in up]
        last = lax.slice_in_dim(x, length - width, length, axis=dim)
        first = lax.slice_in_dim(x, 0, width, axis=dim)
        before = lax.ppermute(last, axis, up)
        after = lax.ppermute(first, axis, down)
        x = jnp.concatenate([before, x, after], axis=dim)
    return x


def surrogate(potential):
    return 1.0 / (1.0 + (math.pi * (potential - 1.0)) ** 2)


def offsets_list():
    return [(row_shift, col_shift) for row_shift in (-1, 0, 1) for col_shift in (-1, 0, 1)]


def on_device(frames, membrane, cotangent, master, moment, second):
    steps_count, samples, rows, cols, chans = frames.shape
    weights = lax.all_gather(master.astype(jnp.bfloat16), "dp", axis=0, tiled=True)
    stacked = jnp.concatenate([membrane[None], frames], axis=0)
    rimmed = extended(stacked, (("space", 2),), 1)
    voltage = rimmed[0].astype(jnp.float32)
    potentials = []
    fired = []
    for position in range(steps_count):
        potential = 0.5 * voltage + rimmed[position + 1].astype(jnp.float32)
        spikes = jnp.where(potential >= 1.0, jnp.float32(1.0), jnp.float32(0.0))
        voltage = potential - spikes
        potentials.append(potential[:, 1:-1])
        fired.append(spikes)
    potential_all = jnp.stack(potentials)
    spike_all = jnp.stack(fired).astype(jnp.bfloat16)
    col_pad = ((0, 0), (0, 0), (0, 0), (1, 1), (0, 0))
    spike_pad = jnp.pad(spike_all, col_pad)
    grad_rim = extended(cotangent, (("space", 2),), 1)
    grad_pad = jnp.pad(grad_rim, col_pad)
    spike_cols = jnp.concatenate(
        [spike_pad[:, :, 1 + a : 1 + a + rows, 1 + b : 1 + b + cols] for a, b in offsets_list()],
        axis=-1,
    ).reshape(-1, 9 * chans)
    grad_cols = jnp.concatenate(
        [grad_pad[:, :, 1 - a : 1 - a + rows, 1 - b : 1 - b + cols] for a, b in offsets_list()],
        axis=-1,
    ).reshape(-1, 9, chans)
    grad_flat = cotangent.reshape(-1, chans)
    weight_local = lax.dot_general(
        spike_cols, grad_flat, (((0,), (0,)), ((), ())), preferred_element_type=jnp.float32
    )
    dspikes = jnp.einsum(
        "nkd,kcd->nc",
        grad_cols,
        weights.reshape(9, chans, chans),
        preferred_element_type=jnp.float32,
    )
    dspikes = dspikes.reshape(steps_count, samples, rows, cols, chans)
    carried = jnp.zeros((samples, rows, cols, chans), jnp.float32)
    outs = [None] * steps_count
    for position in reversed(range(steps_count)):
        carried = dspikes[position] * surrogate(potential_all[position]) + 0.5 * carried
        outs[position] = (cotangent[position].astype(jnp.float32) + carried).astype(jnp.bfloat16)
    grad_input = jnp.stack(outs)
    membrane_grad = 0.5 * carried
    data_count = lax.axis_size("dp")
    total_cells = samples * data_count * lax.axis_size("rep") * rows * lax.axis_size("space") * cols
    shard_part = lax.psum_scatter(weight_local, "dp", scatter_dimension=0, tiled=True)
    summed = lax.psum(shard_part, ("space", "rep"))
    weight_grad = summed * (1.0 / math.sqrt(steps_count * total_cells))
    new_moment = 0.9 * moment + 0.1 * weight_grad
    new_second = 0.95 * second + 0.05 * weight_grad * weight_grad
    update = new_moment / (jnp.sqrt(new_second) + 1e-08)
    return (grad_input, membrane_grad, weight_grad, new_moment, new_second, update)


def solution(mesh):
    return jax.shard_map(
        on_device,
        mesh=mesh,
        in_specs=(
            P(None, ("dp", "rep"), "space", None, None),
            P(("dp", "rep"), "space", None, None),
            P(None, ("dp", "rep"), "space", None, None),
            P("dp", None),
            P("dp", None),
            P("dp", None),
        ),
        out_specs=(
            P(None, ("dp", "rep"), "space", None, None),
            P(("dp", "rep"), "space", None, None),
            P("dp", None),
            P("dp", None),
            P("dp", None),
            P("dp", None),
        ),
        check_vma=False,
    )
```

profile of v0, /device:TPU:0, one launch (start us, length us, event | category | flops | bytes accessed | tf_op | source)
XLA Modules:
  0.0 351.5 jit_solution(18133478292274602957)
XLA Ops:
  7.2 1.1 pad_maximum_fusion.4
  8.3 1.3 collective-permute-start.3
  9.6 3.2 collective-permute-start.2
  12.8 2.8 convert_element_type.357
  15.7 1.8 pad_maximum_fusion
  24.6 10.2 %fusion.4 = f32[4608,512]{1,0:T(8,128)} fusion(bf16[6,1,8,32,4608]{4,3,2,0,1:T(8,128)(2,1)S(1)} %fusion.21, bf16[6,1,8,32,512]{4,3,2,1,0:T(8,128)(2,1)S(1)} %copy-done), kind=kOutput, calls=%fused_computation.4 | convolution fusion | flops 7247757312 | bytes 25165824 | tf_op jit(solution)/shard_map/dot_general | solution.py:58
  34.8 1.1 fusion.104
  35.9 1.3 collective-permute-start.1
  37.2 5.5 %collective-permute-start = (bf16[6,1,1,32,512]{4,3,2,1,0:T(8,128)(2,1)S(1)}, bf16[6,1,1,32,512]{4,3,2,1,0:T(8,128)(2,1)S(1)}, u32[]{:S(2)}, u32[]{:S(2)}) collective-permute-start(bf16[6,1,1,32,512]{4,3,2,1,0:T(8,128)(2,1)S(1)} %get-tuple-element.29), channel_id=1, source_target_pairs={{0,2},{2,4},{4,6},{1,3},{3,5},{5,7},{8,10},{10,12},{12,14},{9,11},... | collective-permute-start | bytes 589832 | tf_op jit(solution)/shard_map/ppermute | solution.py:15
  42.7 0.8 collective-permute-done
  43.5 2.3 fusion.15
  45.9 1.7 slice_dynamic-update-slice_fusion.8
  47.5 1.4 fusion.23
  49.0 1.4 slice_dynamic-update-slice_fusion.7
  50.4 2.1 slice_dynamic-update-slice_fusion.6
  52.5 1.4 constant_dynamic-update-slice_fusion
  53.8 1.4 slice_dynamic-update-slice_fusion.5
  55.2 2.0 slice_dynamic-update-slice_fusion.4
  57.2 1.4 fusion.22
  58.6 1.4 slice_dynamic-update-slice_fusion.3
  60.0 26.6 %reshape.515 = bf16[1536,9,512]{2,1,0:T(8,128)(2,1)} reshape(bf16[6,1,8,32,4608]{4,3,2,1,0:T(8,128)(2,1)} %slice_dynamic-update-slice_fusion.3) | data formatting | bytes 28311552 | tf_op jit(solution)/shard_map/reshape | solution.py:56
  86.6 1.0 fusion.73
  87.6 0.9 convert_bitcast_fusion.1
  88.6 1.8 fusion.28
  90.4 17.5 %all-gather.2.cloned.1.call-done = bf16[4608,512]{1,0:T(8,128)(2,1)} async-done(((bf16[1152,512]{1,0:T(8,128)(2,1)}), bf16[4608,512]{1,0:T(8,128)(2,1)}) %all-gather.2.cloned.1.call-update) | async-done | bytes 4718608 | tf_op jit(solution)/shard_map/all_gather | solution.py:31
  107.9 25.8 %fusion.8 = f32[1536,512]{1,0:T(8,128)S(1)} fusion(bf16[9,512,512]{2,1,0:T(8,128)(2,1)} %bitcast.158, bf16[1536,9,512]{2,1,0:T(8,128)(2,1)} %reshape.515), kind=kOutput, calls=%fused_computation.8 | convolution fusion | flops 7247757312 | bytes 22020096 | tf_op jit(solution)/shard_map/nkd,kcd->nc/dot_general | solution.py:61
  135.8 1.7 broadcast_multiply_fusion.1
  138.3 131.7 %reduce-scatter.2.cloned.1.call-done = f32[1152,512]{1,0:T(8,128)} async-done(((f32[4608,512]{1,0:T(8,128)}), f32[1152,512]{1,0:T(8,128)}) %reduce-scatter.2.cloned.1.call-update) | async-done | bytes 2359312 | tf_op jit(solution)/shard_map/reduce_scatter | solution.py:77
  270.1 2.2 fusion.87
  273.9 0.9 fusion.93
  275.6 61.5 %all-reduce.4.cloned.1.call-done = f32[1152,512]{1,0:T(8,128)} async-done(((f32[1152,512]{1,0:T(8,128)}), f32[1152,512]{1,0:T(8,128)}) %all-reduce.4.cloned.1.call-update) | async-done | bytes 2359312 | tf_op jit(solution)/shard_map/psum | solution.py:78
  337.1 7.9 %add_divide_fusion = (f32[1152,512]{1,0:T(8,128)}, f32[1152,512]{1,0:T(8,128)}, f32[1152,512]{1,0:T(8,128)}, f32[1152,512]{1,0:T(8,128)}) fusion(f32[1152,512]{1,0:T(8,128)} %all-reduce.4.cloned.1.call-done, f32[1152,512]{1,0:T(8,128)} %param.11, f32[1152,512]{1,0:T(8,128)} %param.10), kind=kLoop, calls=%fused_computation.14 | loop fusion | flops 5898240 | bytes 16515072 | tf_op jit(solution)/shard_map/div | solution.py:82
  (55 shorter events, 12.3 us)
Async XLA Ops:
  7.2 100.7 %all-gather.2.cloned.1.call-start = ((), (), s32[]{:S(2)}) async-start(), calls=%async_computation.1 | async-start | bytes 5898240 | tf_op jit(solution)/shard_map/all_gather | solution.py:31
  8.3 7.4 %collective-permute-start.3 = (bf16[7,1,1,32,512]{4,3,2,1,0:T(8,128)(2,1)S(1)}, bf16[7,1,1,32,512]{4,3,2,1,0:T(8,128)(2,1)S(1)}, u32[]{:S(2)}, u32[]{:S(2)}) collective-permute-start(bf16[7,1,1,32,512]{4,3,2,1,0:T(8,128)(2,1)S(1)} %get-tuple-element.28), channel_id=1, source_target_pairs={{2,0},{4,2},{6,4},{3,1},{5,3},{7,5},{10,8},{12,10},{14,12},{11,9},... | collective-permute-start | bytes 688136 | tf_op jit(solution)/shard_map/ppermute | solution.py:16
  9.6 6.1 %copy-start.12 = (bf16[1,8,32,512]{3,2,1,0:T(8,128)(2,1)S(1)}, bf16[1,8,32,512]{3,2,1,0:T(8,128)(2,1)}, u32[]{:S(2)}) copy-start(bf16[1,8,32,512]{3,2,1,0:T(8,128)(2,1)} %param.7) | copy-start | bytes 786436
  9.6 6.1 %collective-permute-start.2 = (bf16[7,1,1,32,512]{4,3,2,1,0:T(8,128)(2,1)S(1)}, bf16[7,1,1,32,512]{4,3,2,1,0:T(8,128)(2,1)S(1)}, u32[]{:S(2)}, u32[]{:S(2)}) collective-permute-start(bf16[7,1,1,32,512]{4,3,2,1,0:T(8,128)(2,1)S(1)} %get-tuple-element.27), channel_id=1, source_target_pairs={{0,2},{2,4},{4,6},{1,3},{3,5},{5,7},{8,10},{10,12},{12,14},{9,11},... | collective-permute-start | bytes 688136 | tf_op jit(solution)/shard_map/ppermute | solution.py:15
  15.6 254.4 %reduce-scatter.2.cloned.1.call-start = ((), (), s32[]{:S(2)}) async-start(), calls=%async_computation.2 | async-start | bytes 11796480 | tf_op jit(solution)/shard_map/reduce_scatter | solution.py:77
  23.2 1.4 copy-start
  34.8 302.3 %all-reduce.4.cloned.1.call-start = ((), (), s32[]{:S(2)}) async-start(), calls=%async_computation.3 | async-start | bytes 4718592 | tf_op jit(solution)/shard_map/psum | solution.py:78
  35.9 6.8 %collective-permute-start.1 = (bf16[6,1,1,32,512]{4,3,2,1,0:T(8,128)(2,1)S(1)}, bf16[6,1,1,32,512]{4,3,2,1,0:T(8,128)(2,1)S(1)}, u32[]{:S(2)}, u32[]{:S(2)}) collective-permute-start(bf16[6,1,1,32,512]{4,3,2,1,0:T(8,128)(2,1)S(1)} %get-tuple-element.30), channel_id=1, source_target_pairs={{2,0},{4,2},{6,4},{3,1},{5,3},{7,5},{10,8},{12,10},{14,12},{11,9},... | collective-permute-start | bytes 589832 | tf_op jit(solution)/shard_map/ppermute | solution.py:16
  37.2 6.3 %collective-permute-start = (bf16[6,1,1,32,512]{4,3,2,1,0:T(8,128)(2,1)S(1)}, bf16[6,1,1,32,512]{4,3,2,1,0:T(8,128)(2,1)S(1)}, u32[]{:S(2)}, u32[]{:S(2)}) collective-permute-start(bf16[6,1,1,32,512]{4,3,2,1,0:T(8,128)(2,1)S(1)} %get-tuple-element.29), channel_id=1, source_target_pairs={{0,2},{2,4},{4,6},{1,3},{3,5},{5,7},{8,10},{10,12},{12,14},{9,11},... | collective-permute-start | bytes 589832 | tf_op jit(solution)/shard_map/ppermute | solution.py:15
  45.8 1.7 copy-start.1
  133.7 1.1 copy-start.4
  133.7 1.3 copy-start.6
  133.7 1.5 copy-start.7
  133.8 1.7 copy-start.8
  133.8 1.8 copy-start.9
  133.8 2.0 copy-start.10
  135.8 1.7 copy-start.2
  270.1 2.3 copy-start.3
  270.1 3.0 copy-start.11
  270.1 3.8 %copy-start.5 = (f32[1,10,32,512]{3,2,1,0:T(8,128)S(1)}, f32[1,10,32,512]{3,2,1,0:T(8,128)}, u32[]{:S(2)}) copy-start(f32[1,10,32,512]{3,2,1,0:T(8,128)} %get-tuple-element.17) | copy-start | bytes 1966084
Sparse Core Ops, SparseCore 0:
  15.8 92.1 all-gather.1
  110.3 159.7 reduce-scatter.1
  273.3 63.7 all-reduce.3
where the time goes:
time: 353 us; the launch traced here: 352 us
  waiting for transfers between devices  212 us (60%)
  local copies, waits for them, and re-layouts  46.2 us (13%)
  matrix products  36 us (10%)
  other arithmetic  32.3 us (9%)
  between operations  14.1 us (4%)
  starting transfers between devices  11.3 us (3%)
    reduce_scatter x1, waiting for transfers between devices, on_device(): lax.psum_scatter(weight_local, 'dp', scatter_dimension=0, tiled=True)  132 us
    psum x1, waiting for transfers between devices, on_device(): summed = lax.psum(shard_part, ('space', 'rep'))  61.5 us
    reshape x1, local copies, waits for them, and re-layouts, on_device(): grad_cols = jnp.concatenate([grad_pad[:, :, 1 - a:1 - a + rows, 1 - b:1 -...  26.6 us
    dot_general x1, matrix products, on_device(): jnp.einsum('nkd,kcd->nc', grad_cols, weights.reshape(9, chans, chans), pr...  25.8 us
    all_gather x1, waiting for transfers between devices, on_device(): lax.all_gather(master.astype(jnp.bfloat16), 'dp', axis=0, tiled=True)  17.5 us
    unnamed x40, local copies, waits for them, and re-layouts  16.1 us
    dot_general x1, matrix products, on_device(): lax.dot_general(spike_cols, grad_flat, (((0,), (0,)), ((), ())), preferre...  10.2 us
    unnamed x12, other arithmetic  9.82 us
  transfers between devices with their start and end apart: 7, of which 4 were waited for; matrix products, arithmetic and copies ran while one was open for 29% of the time, Pallas kernels for 0%

commit v1 on v0

--- a/solution.py
+++ b/solution.py
@@ -3,6 +3,11 @@
 import jax.numpy as jnp
 from jax import lax
 from jax.sharding import PartitionSpec as P
+
+
+def add_all(x, axis):
+    terms = lax.all_gather(x, axis)
+    return jnp.sum(terms, axis=0)
 
 
 def extended(x, sides, width):
@@ -75,7 +80,7 @@
     data_count = lax.axis_size("dp")
     total_cells = samples * data_count * lax.axis_size("rep") * rows * lax.axis_size("space") * cols
     shard_part = lax.psum_scatter(weight_local, "dp", scatter_dimension=0, tiled=True)
-    summed = lax.psum(shard_part, ("space", "rep"))
+    summed = add_all(shard_part, ("space", "rep"))
     weight_grad = summed * (1.0 / math.sqrt(steps_count * total_cells))
     new_moment = 0.9 * moment + 0.1 * weight_grad
     new_second = 0.95 * second + 0.05 * weight_grad * weight_grad

time: 353 us -> 417 us (1.18)
  waiting for transfers between devices: 212 us -> 271 us
  other arithmetic: 32.3 us -> 39.8 us
    all_gather x0 -> x1, waiting for transfers between devices: none -> 64.8 us  [add_all(): terms = lax.all_gather(x, axis)]
    psum x1 -> x0, waiting for transfers between devices: 61.5 us -> none  [on_device(): summed = lax.psum(shard_part, ('space', 'rep'))]
    reduce_scatter x1, waiting for transfers between devices: 132 us -> 165 us  [on_device(): lax.psum_scatter(weight_local, 'dp', scatter_dimension=0, tiled=True)]
    all_gather x1, waiting for transfers between devices: 17.5 us -> 39.2 us  [on_device(): lax.all_gather(master.astype(jnp.bfloat16), 'dp', axis=0, tiled=True)]
    reduce_sum x0 -> x1, other arithmetic: none -> 10.4 us  [add_all(): return jnp.sum(terms, axis=0)]
    unnamed x40 -> x34, local copies, waits for them, and re-layouts: 16.1 us -> 16 us
  transfers between devices with their start and end apart: 7 -> 7, of which waited for: 4 -> 5; matrix products, arithmetic and copies ran while one was open for 29% -> 20% of each run, Pallas kernels for 0% -> 0%
where the time goes in v1:
time: 417 us; the launch traced here: 416 us
  waiting for transfers between devices  271 us (65%)
  local copies, waits for them, and re-layouts  46.1 us (11%)
  other arithmetic  39.8 us (10%)
  matrix products  35.9 us (9%)
  between operations  14 us (3%)
  starting transfers between devices  8.97 us (2%)
    reduce_scatter x1, waiting for transfers between devices, on_device(): lax.psum_scatter(weight_local, 'dp', scatter_dimension=0, tiled=True)  165 us
    all_gather x1, waiting for transfers between devices, add_all(): terms = lax.all_gather(x, axis)  64.8 us
    all_gather x1, waiting for transfers between devices, on_device(): lax.all_gather(master.astype(jnp.bfloat16), 'dp', axis=0, tiled=True)  39.2 us
    reshape x1, local copies, waits for them, and re-layouts, on_device(): grad_cols = jnp.concatenate([grad_pad[:, :, 1 - a:1 - a + rows, 1 - b:1 -...  26.6 us
    dot_general x1, matrix products, on_device(): jnp.einsum('nkd,kcd->nc', grad_cols, weights.reshape(9, chans, chans), pr...  25.8 us
    unnamed x34, local copies, waits for them, and re-layouts  16 us
    reduce_sum x1, other arithmetic, add_all(): return jnp.sum(terms, axis=0)  10.4 us
    dot_general x1, matrix products, on_device(): lax.dot_general(spike_cols, grad_flat, (((0,), (0,)), ((), ())), preferre...  10.1 us
  transfers between devices with their start and end apart: 7, of which 5 were waited for; matrix products, arithmetic and copies ran while one was open for 20% of the time, Pallas kernels for 0%

profile of v1, /device:TPU:0, one launch (start us, length us, event | category | flops | bytes accessed | tf_op | source)
XLA Modules:
  0.0 415.8 jit_solution(10228255993633196208)
XLA Ops:
  7.2 1.2 pad_maximum_fusion.4
  8.4 1.3 collective-permute-start.3
  9.7 3.0 collective-permute-start.2
  12.8 1.1 collective-permute-done.2
  21.3 10.1 %fusion.4 = f32[4608,512]{1,0:T(8,128)} fusion(bf16[6,1,8,32,4608]{4,3,2,0,1:T(8,128)(2,1)S(1)} %fusion.21, bf16[6,1,8,32,512]{4,3,2,1,0:T(8,128)(2,1)S(1)} %copy-done), kind=kOutput, calls=%fused_computation.4 | convolution fusion | flops 7247757312 | bytes 25165824 | tf_op jit(solution)/shard_map/dot_general | solution.py:63
  31.5 2.8 convert_element_type.357
  34.4 165.0 %reduce-scatter.2.cloned.1.call-done = f32[1152,512]{1,0:T(8,128)} async-done(((f32[4608,512]{1,0:T(8,128)}), f32[1152,512]{1,0:T(8,128)}) %reduce-scatter.2.cloned.1.call-update) | async-done | bytes 2359312 | tf_op jit(solution)/shard_map/reduce_scatter | solution.py:82
  199.5 1.1 fusion.104
  200.5 1.3 collective-permute-start.1
  201.8 3.2 collective-permute-start
  205.9 2.3 fusion.15
  208.2 1.7 slice_dynamic-update-slice_fusion.8
  210.0 1.5 fusion.23
  211.5 1.4 slice_dynamic-update-slice_fusion.7
  212.9 2.0 slice_dynamic-update-slice_fusion.6
  214.9 1.4 constant_dynamic-update-slice_fusion
  216.3 1.5 slice_dynamic-update-slice_fusion.5
  217.8 2.0 slice_dynamic-update-slice_fusion.4
  219.8 1.4 fusion.22
  221.2 1.4 slice_dynamic-update-slice_fusion.3
  222.6 26.6 %reshape.515 = bf16[1536,9,512]{2,1,0:T(8,128)(2,1)} reshape(bf16[6,1,8,32,4608]{4,3,2,1,0:T(8,128)(2,1)} %slice_dynamic-update-slice_fusion.3) | data formatting | bytes 28311552 | tf_op jit(solution)/shard_map/reshape | solution.py:61
  249.2 0.9 fusion.73
  250.2 0.9 convert_bitcast_fusion.1
  251.1 1.6 fusion.28
  252.7 39.2 %all-gather.4.cloned.1.call-done = bf16[4608,512]{1,0:T(8,128)(2,1)} async-done(((bf16[1152,512]{1,0:T(8,128)(2,1)}), bf16[4608,512]{1,0:T(8,128)(2,1)}) %all-gather.4.cloned.1.call-update) | async-done | bytes 4718608 | tf_op jit(solution)/shard_map/all_gather | solution.py:36
  291.9 25.8 %fusion.8 = f32[1536,512]{1,0:T(8,128)S(1)} fusion(bf16[9,512,512]{2,1,0:T(8,128)(2,1)} %bitcast.160, bf16[1536,9,512]{2,1,0:T(8,128)(2,1)} %reshape.515), kind=kOutput, calls=%fused_computation.8 | convolution fusion | flops 7247757312 | bytes 22020096 | tf_op jit(solution)/shard_map/nkd,kcd->nc/dot_general | solution.py:66
  319.6 1.7 broadcast_multiply_fusion.1
  322.1 0.9 fusion.87
  324.5 0.9 fusion.93
  326.2 64.8 %all-gather.6.cloned.1.call-done = f32[9216,512]{1,0:T(8,128)} async-done(((f32[1152,512]{1,0:T(8,128)}), f32[9216,512]{1,0:T(8,128)}) %all-gather.6.cloned.1.call-update) | async-done | bytes 18874384 | tf_op jit(solution)/shard_map/all_gather | solution.py:9
  391.0 10.4 %reduce_sum.9 = f32[1152,512]{1,0:T(8,128)} reduce(f32[8,1152,512]{2,1,0:T(8,128)} %bitcast.149, f32[]{:T(128)} %constant.28.clone.1), dimensions={0}, to_apply=%region_1.2 | reduce | flops 4128768 | bytes 21233668 | tf_op jit(solution)/shard_map/reduce_sum | solution.py:10
  401.4 7.9 %add_divide_fusion = (f32[1152,512]{1,0:T(8,128)}, f32[1152,512]{1,0:T(8,128)}, f32[1152,512]{1,0:T(8,128)}, f32[1152,512]{1,0:T(8,128)}) fusion(f32[1152,512]{1,0:T(8,128)} %reduce_sum.9, f32[1152,512]{1,0:T(8,128)} %param.11, f32[1152,512]{1,0:T(8,128)} %param.10), kind=kLoop, calls=%fused_computation.14 | loop fusion | flops 5898240 | bytes 16515072 | tf_op jit(solution)/shard_map/div | solution.py:87
  (50 shorter events, 13.3 us)
Async XLA Ops:
  7.2 6.7 %copy-start.9 = (bf16[1,8,32,512]{3,2,1,0:T(8,128)(2,1)S(1)}, bf16[1,8,32,512]{3,2,1,0:T(8,128)(2,1)}, u32[]{:S(2)}) copy-start(bf16[1,8,32,512]{3,2,1,0:T(8,128)(2,1)} %param.7) | copy-start | bytes 786436
  7.2 192.3 %reduce-scatter.2.cloned.1.call-start = ((), (), s32[]{:S(2)}) async-start(), calls=%async_computation.2 | async-start | bytes 11796480 | tf_op jit(solution)/shard_map/reduce_scatter | solution.py:82
  7.2 6.6 %copy-start.3 = (bf16[6,1,8,32,512]{4,3,2,1,0:T(8,128)(2,1)S(1)}, bf16[6,1,8,32,512]{4,3,2,1,0:T(8,128)(2,1)}, u32[]{:S(2)}) copy-start(bf16[6,1,8,32,512]{4,3,2,1,0:T(8,128)(2,1)} %param.6) | copy-start | bytes 4718596
  8.4 4.4 %collective-permute-start.3 = (bf16[7,1,1,32,512]{4,3,2,1,0:T(8,128)(2,1)S(1)}, bf16[7,1,1,32,512]{4,3,2,1,0:T(8,128)(2,1)S(1)}, u32[]{:S(2)}, u32[]{:S(2)}) collective-permute-start(bf16[7,1,1,32,512]{4,3,2,1,0:T(8,128)(2,1)S(1)} %get-tuple-element.28), channel_id=1, source_target_pairs={{2,0},{4,2},{6,4},{3,1},{5,3},{7,5},{10,8},{12,10},{14,12},{11,9},... | collective-permute-start | bytes 688136 | tf_op jit(solution)/shard_map/ppermute | solution.py:21
  9.7 4.1 collective-permute-start.2
  19.9 1.4 copy-start
  31.5 260.4 %all-gather.4.cloned.1.call-start = ((), (), s32[]{:S(2)}) async-start(), calls=%async_computation.1 | async-start | bytes 5898240 | tf_op jit(solution)/shard_map/all_gather | solution.py:36
  34.4 356.6 %all-gather.6.cloned.1.call-start = ((), (), s32[]{:S(2)}) async-start(), calls=%async_computation.3 | async-start | bytes 21233664 | tf_op jit(solution)/shard_map/all_gather | solution.py:9
  200.5 4.5 %collective-permute-start.1 = (bf16[6,1,1,32,512]{4,3,2,1,0:T(8,128)(2,1)S(1)}, bf16[6,1,1,32,512]{4,3,2,1,0:T(8,128)(2,1)S(1)}, u32[]{:S(2)}, u32[]{:S(2)}) collective-permute-start(bf16[6,1,1,32,512]{4,3,2,1,0:T(8,128)(2,1)S(1)} %get-tuple-element.30), channel_id=1, source_target_pairs={{2,0},{4,2},{6,4},{3,1},{5,3},{7,5},{10,8},{12,10},{14,12},{11,9},... | collective-permute-start | bytes 589832 | tf_op jit(solution)/shard_map/ppermute | solution.py:21
  201.8 4.1 collective-permute-start
  208.2 1.8 copy-start.1
  317.7 1.1 copy-start.4
  317.7 1.3 copy-start.5
  317.7 1.5 copy-start.6
  317.7 1.7 copy-start.7
  317.7 1.8 copy-start.8
  319.5 1.7 copy-start.2
Sparse Core Ops, SparseCore 0:
  31.6 167.7 reduce-scatter.1
  201.6 90.2 all-gather.3
  293.7 97.1 all-gather.5
